TPU v7x, 256 devices: a whole 4x4x8 slice. The times are simulated.
256 devices in a mesh: gx: 32 (over x, z), gy: 8 (over y, core).
Axes of the slice: x: 4, y: 4, z: 8, core: 2. Of those that a mesh axis runs over, the one named last changes fastest.
Arguments:
- field: bfloat16 [3, 1, 48, 256, 1024], P(None, None, None, 'gx', 'gy'), may hold values from -6 to 6
- weight_x: bfloat16 [15, 48, 48], replicated, may hold values from -0.21875 to 0.21875
- weight_y: bfloat16 [15, 48, 48], replicated, may hold values from -0.21875 to 0.21875
- cotangent: bfloat16 [3, 1, 48, 256, 1024], P(None, None, None, 'gx', 'gy'), may hold values from -6 to 6
Outputs:
- output: bfloat16 [3, 1, 48, 256, 1024], P(None, None, None, 'gx', 'gy')
- field_grad: bfloat16 [3, 1, 48, 256, 1024], P(None, None, None, 'gx', 'gy')
- wx_grad: float32 [15, 48, 48], replicated
- wy_grad: float32 [15, 48, 48], replicated
All inputs are finite; a program needn't handle non-finite values.
Results may differ from a plain program's by a relative error of at most 0.0054.
Values may be sent and summed in bfloat16 or wider, within the bound.
No kernel may reach another device: no remote copies, remote signals or barrier semaphores. Data moves between devices by JAX's collectives and lax.ppermute only.
A program may use at most 64 MiB of HBM per device.

v0:
```python
import jax
import jax.numpy as jnp
from jax import lax
from jax.sharding import PartitionSpec as P


def with_halo(cells, sides, width):
    for axis, dim in sides:
        count = lax.axis_size(axis)
        ends = count - 1
        head = lax.slice_in_dim(cells, 0, width, axis=dim)
        tail = lax.slice_in_dim(cells, cells.shape[dim] - width, cells.shape[dim], axis=dim)
        cells = jnp.concatenate(
            [
                lax.ppermute(tail, axis, [(i, (i + 1) % count) for i in range(ends)]),
                cells,
                lax.ppermute(head, axis, [((i + 1) % count, i) for i in range(ends)]),
            ],
            axis=dim,
        )
    return cells


def conv_padded(padded, weight, dim):
    taps = weight.shape[0]
    length = padded.shape[dim] - taps + 1
    total = None
    for tap in range(taps):
        piece = lax.slice_in_dim(padded, tap, tap + length, axis=dim)
        term = jnp.einsum("bzcxy,co->bzoxy", piece, weight[tap], preferred_element_type=jnp.float32)
        total = term if total is None else total + term
    return total


def flipped(weight):
    return jnp.transpose(jnp.flip(weight, 0), (0, 2, 1))


def tap_products(padded, grads, taps, dim):
    length = grads.shape[dim]
    terms = []
    for tap in range(taps):
        piece = lax.slice_in_dim(padded, tap, tap + length, axis=dim)
        terms.append(
            jnp.einsum("bzcxy,bzoxy->co", piece, grads, preferred_element_type=jnp.float32)
        )
    return jnp.stack(terms)


def activate(pre):
    return jax.nn.gelu(pre.astype(jnp.float32)).astype(jnp.bfloat16)


def y_reach(values, half):
    return with_halo(values, (("gy", 4),), half)


def per_device(field, weight_x, weight_y, cotangent):
    taps = weight_x.shape[0]
    half = (taps - 1) // 2
    lines = lax.all_to_all(field, "gx", split_axis=4, concat_axis=3, tiled=True)
    lines_pad = jnp.pad(lines, ((0, 0), (0, 0), (0, 0), (half, half), (0, 0)))
    pre_lines = lax.optimization_barrier(conv_padded(lines_pad, weight_x, 3).astype(jnp.bfloat16))
    act_lines = activate(pre_lines)
    act, pre = (
        lax.all_to_all(act_lines, "gx", split_axis=3, concat_axis=4, tiled=True),
        lax.all_to_all(pre_lines, "gx", split_axis=3, concat_axis=4, tiled=True),
    )
    act_pad = y_reach(act, half)
    output = (field.astype(jnp.float32) + conv_padded(act_pad, weight_y, 4)).astype(jnp.bfloat16)
    grad_pad = y_reach(cotangent, half)
    act_grad = conv_padded(grad_pad, flipped(weight_y), 4)
    _, pull = jax.vjp(jax.nn.gelu, pre.astype(jnp.float32))
    pre_grad = pull(act_grad)[0].astype(jnp.bfloat16)
    wy_term = tap_products(act_pad, cotangent, taps, 4)
    paired = with_halo(jnp.stack((field, pre_grad)), (("gx", 4),), half)
    field_pad = paired[0]
    grad_xpad = paired[1]
    field_grad = (
        cotangent.astype(jnp.float32) + conv_padded(grad_xpad, flipped(weight_x), 3)
    ).astype(jnp.bfloat16)
    wx_term = tap_products(field_pad, pre_grad, taps, 3)
    wx_sum, wy_sum = lax.psum((wx_term, wy_term), ("gx", "gy"))
    count = (
        field.shape[0]
        * field.shape[1]
        * field.shape[3]
        * field.shape[4]
        * lax.axis_size("gx")
        * lax.axis_size("gy")
    )
    factor = 1.0 / jnp.sqrt(jnp.float32(count))
    return (output, field_grad, wx_sum * factor, wy_sum * factor)


def solution(mesh):
    in_specs = (P(None, None, None, "gx", "gy"), P(), P(), P(None, None, None, "gx", "gy"))
    out_specs = (P(None, None, None, "gx", "gy"), P(None, None, None, "gx", "gy"), P(), P())
    return jax.shard_map(
        per_device, mesh=mesh, in_specs=in_specs, out_specs=out_specs, check_vma=False
    )
```

profile of v0, /device:TPU:8, one launch (start us, length us, event | category | flops | bytes accessed | tf_op | source)
XLA Modules:
  0.0 378.1 jit_solution(10416243189057325038)
XLA Ops:
  7.2 1.6 copy.144
  8.8 1.7 reshape.644
  10.5 11.3 %all-to-all-start = ((bf16[32,2,2304]{2,1,0:T(2,128)(2,1)}), bf16[32,2,2304]{2,1,0:T(2,128)(2,1)S(1)}, u32[]{:S(2)}, u32[]{:S(2)}) async-start(bf16[32,2,2304]{2,1,0:T(2,128)(2,1)} %reshape.644), calls=%async_computation | async-start | bytes 589824 | tf_op jit(solution)/shard_map/all_to_all | solution.py:61
  22.1 1.9 collective-permute-start.3
  24.0 2.4 collective-permute-start.2
  26.7 0.7 reverse_bitcast_fusion
  27.4 0.8 copy.389
  28.1 3.9 %collective-permute-done.2 = bf16[3,1,48,8,7]{4,2,3,0,1:T(8,128)(2,1)S(1)} collective-permute-done((bf16[3,1,48,8,7]{4,2,3,0,1:T(8,128)(2,1)S(1)}, bf16[3,1,48,8,7]{4,2,3,0,1:T(8,128)(2,1)S(1)}, u32[]{:S(2)}, u32[]{:S(2)}) %collective-permute-start.2) | collective-permute-done | bytes 16160 | tf_op jit(solution)/shard_map/ppermute | solution.py:15
  35.1 1.1 fusion.6
  36.2 0.8 reshape.645
  39.8 0.4 convolution_add_fusion.39
  42.6 0.6 copy.165
  43.2 1.7 reshape.646
  44.9 10.0 %all-to-all-start.1 = ((bf16[32,2,2304]{2,1,0:T(2,128)(2,1)}), bf16[32,2,2304]{2,1,0:T(2,128)(2,1)S(1)}, u32[]{:S(2)}, u32[]{:S(2)}) async-start(bf16[32,2,2304]{2,1,0:T(2,128)(2,1)} %reshape.646), calls=%async_computation.1 | async-start | bytes 589824 | tf_op jit(solution)/shard_map/all_to_all | solution.py:66
  54.9 1.0 fusion.5
  55.9 1.0 fusion.4
  56.9 1.0 fusion.3
  57.9 0.6 copy.196
  58.5 1.7 reshape.648
  60.2 6.9 %all-to-all-done.1 = bf16[32,2,2304]{2,1,0:T(2,128)(2,1)S(1)} async-done(((bf16[32,2,2304]{2,1,0:T(2,128)(2,1)}), bf16[32,2,2304]{2,1,0:T(2,128)(2,1)S(1)}, u32[]{:S(2)}, u32[]{:S(2)}) %all-to-all-start.1) | async-done | bytes 294944 | tf_op jit(solution)/shard_map/all_to_all | solution.py:66
  67.1 4.7 %all-to-all-start.2 = ((bf16[32,2,2304]{2,1,0:T(2,128)(2,1)}), bf16[32,2,2304]{2,1,0:T(2,128)(2,1)S(1)}, u32[]{:S(2)}, u32[]{:S(2)}) async-start(bf16[32,2,2304]{2,1,0:T(2,128)(2,1)} %reshape.648), calls=%async_computation.2 | async-start | bytes 589824 | tf_op jit(solution)/shard_map/all_to_all | solution.py:67
  71.9 1.9 fusion.2
  73.7 0.8 reshape.647
  74.8 0.5 copy.168
  75.3 0.5 copy.179
  75.8 0.9 fusion.299
  76.7 1.9 collective-permute-start.1
  78.6 2.4 collective-permute-start
  81.0 1.1 fusion.178
  82.1 1.3 all-to-all-done.2
  83.4 0.8 reshape.649
  84.6 1.3 copy.202
  85.9 1.9 fusion.65
  87.9 3.8 %collective-permute-start.4 = (bf16[2,3,1,48,7,128]{5,3,4,1,2,0:T(8,128)(2,1)S(1)}, bf16[2,3,1,48,7,128]{5,3,4,1,2,0:T(8,128)(2,1)S(1)}, u32[]{:S(2)}, u32[]{:S(2)}) collective-permute-start(bf16[2,3,1,48,7,128]{5,3,4,1,2,0:T(8,128)(2,1)S(1)} %get-tuple-element.20), channel_id=1, source_target_pairs={{0,8},{8,16},{16,24},{24,32},{32,40},{40,48},{48,56},{56,64},{64,7... | collective-permute-start | bytes 1548296 | tf_op jit(solution)/shard_map/ppermute | solution.py:15
  91.7 1.5 collective-permute-start.5
  96.0 0.4 fusion.185
  100.4 0.4 convolution_add_fusion.26
  100.8 0.4 convolution_add_fusion.25
  101.2 0.4 convolution_add_fusion.24
  101.6 0.4 convolution_add_fusion.23
  102.0 0.4 convolution_add_fusion.22
  102.9 0.4 fusion.23
  103.7 0.8 copy.220
  105.2 0.7 copy-done.13
  105.9 0.6 collective-permute-done.5
  113.8 0.8 copy.221
  114.6 254.6 %all-reduce.4.cloned.1.call-done = (f32[15,48,48]{2,1,0:T(8,128)}, f32[15,48,48]{2,1,0:T(8,128)}) async-done(((f32[15,48,48]{2,1,0:T(8,128)}, f32[15,48,48]{2,1,0:T(8,128)}), (f32[15,48,48]{2,1,0:T(8,128)}, f32[15,48,48]{2,1,0:T(8,128)})) %all-reduce.4.cloned.1.call-update) | async-done | bytes 276496 | tf_op jit(solution)/shard_map/psum | solution.py:83
  369.2 2.0 broadcast_multiply_fusion
  (126 shorter events, 24.5 us)
Async XLA Ops:
  7.2 14.7 %copy-start = (bf16[3,1,48,8,128]{4,3,2,1,0:T(8,128)(2,1)S(1)}, bf16[3,1,48,8,128]{4,3,2,1,0:T(8,128)(2,1)}, u32[]{:S(2)}) copy-start(bf16[3,1,48,8,128]{4,3,2,1,0:T(8,128)(2,1)} %param.7) | copy-start | bytes 884740
  8.8 17.7 %copy-start.9 = (bf16[15,48,48]{2,1,0:T(8,128)(2,1)S(1)}, bf16[15,48,48]{2,1,0:T(8,128)(2,1)}, u32[]{:S(2)}) copy-start(bf16[15,48,48]{2,1,0:T(8,128)(2,1)} %param.6) | copy-start | bytes 207364
  10.5 25.7 %all-to-all-start = ((bf16[32,2,2304]{2,1,0:T(2,128)(2,1)}), bf16[32,2,2304]{2,1,0:T(2,128)(2,1)S(1)}, u32[]{:S(2)}, u32[]{:S(2)}) async-start(bf16[32,2,2304]{2,1,0:T(2,128)(2,1)} %reshape.644), calls=%async_computation | async-start | bytes 589824 | tf_op jit(solution)/shard_map/all_to_all | solution.py:61
  21.8 4.9 %copy-start.8 = (bf16[15,48,48]{2,1,0:T(8,128)(2,1)S(1)}, bf16[15,48,48]{2,1,0:T(8,128)(2,1)}, u32[]{:S(2)}) copy-start(bf16[15,48,48]{2,1,0:T(8,128)(2,1)} %param.5) | copy-start | bytes 207364
  21.9 5.5 %copy-start.2 = (bf16[3,1,48,8,128]{4,3,2,1,0:T(8,128)(2,1)S(1)}, bf16[3,1,48,8,128]{4,3,2,1,0:T(8,128)(2,1)}, u32[]{:S(2)}) copy-start(bf16[3,1,48,8,128]{4,3,2,1,0:T(8,128)(2,1)} %param.4) | copy-start | bytes 884740
  22.1 12.6 %collective-permute-start.3 = (bf16[3,1,48,8,7]{4,2,3,0,1:T(8,128)(2,1)S(1)}, bf16[3,1,48,8,7]{4,2,3,0,1:T(8,128)(2,1)S(1)}, u32[]{:S(2)}, u32[]{:S(2)}) collective-permute-start(bf16[3,1,48,8,7]{4,2,3,0,1:T(8,128)(2,1)S(1)} %get-tuple-element.22), channel_id=1, source_target_pairs={{1,0},{2,1},{3,2},{4,3},{5,4},{6,5},{7,6},{9,8},{10,9},{11,10},{12... | collective-permute-start | bytes 48392 | tf_op jit(solution)/shard_map/ppermute | solution.py:17
  24.0 8.0 %collective-permute-start.2 = (bf16[3,1,48,8,7]{4,2,3,0,1:T(8,128)(2,1)S(1)}, bf16[3,1,48,8,7]{4,2,3,0,1:T(8,128)(2,1)S(1)}, u32[]{:S(2)}, u32[]{:S(2)}) collective-permute-start(bf16[3,1,48,8,7]{4,2,3,0,1:T(8,128)(2,1)S(1)} %get-tuple-element.23), channel_id=1, source_target_pairs={{0,1},{1,2},{2,3},{3,4},{4,5},{5,6},{6,7},{8,9},{9,10},{10,11},{11... | collective-permute-start | bytes 48392 | tf_op jit(solution)/shard_map/ppermute | solution.py:15
  26.5 8.6 %copy-start.12 = (bf16[15,48,48]{1,2,0:T(8,128)(2,1)}, bf16[15,48,48]{1,2,0:T(8,128)(2,1)S(1)}, u32[]{:S(2)}) copy-start(bf16[15,48,48]{1,2,0:T(8,128)(2,1)S(1)} %reverse_bitcast_fusion.1) | copy-start | bytes 207364
  42.4 12.5 %copy-start.5 = (f32[48,3,8,128]{3,0,2,1:T(8,128)S(1)}, f32[48,3,8,128]{3,0,2,1:T(8,128)}, u32[]{:S(2)}) copy-start(f32[48,3,8,128]{3,0,2,1:T(8,128)} %fusion.6) | copy-start | bytes 1769476
  44.9 22.2 %all-to-all-start.1 = ((bf16[32,2,2304]{2,1,0:T(2,128)(2,1)}), bf16[32,2,2304]{2,1,0:T(2,128)(2,1)S(1)}, u32[]{:S(2)}, u32[]{:S(2)}) async-start(bf16[32,2,2304]{2,1,0:T(2,128)(2,1)} %reshape.646), calls=%async_computation.1 | async-start | bytes 589824 | tf_op jit(solution)/shard_map/all_to_all | solution.py:66
  67.1 16.3 %all-to-all-start.2 = ((bf16[32,2,2304]{2,1,0:T(2,128)(2,1)}), bf16[32,2,2304]{2,1,0:T(2,128)(2,1)S(1)}, u32[]{:S(2)}, u32[]{:S(2)}) async-start(bf16[32,2,2304]{2,1,0:T(2,128)(2,1)} %reshape.648), calls=%async_computation.2 | async-start | bytes 589824 | tf_op jit(solution)/shard_map/all_to_all | solution.py:67
  71.8 297.4 %all-reduce.4.cloned.1.call-start = ((), (), s32[]{:S(2)}) async-start(), calls=%async_computation.3 | async-start | bytes 1474560 | tf_op jit(solution)/shard_map/psum | solution.py:83
  74.8 6.2 %copy-start.10 = (bf16[15,48,48]{2,1,0:T(8,128)(2,1)S(1)}, bf16[15,48,48]{2,1,0:T(8,128)(2,1)}, u32[]{:S(2)}) copy-start(bf16[15,48,48]{2,1,0:T(8,128)(2,1)} %param.6) | copy-start | bytes 207364
  75.8 8.4 %copy-start.6 = (bf16[3,48,8,128]{3,1,2,0:T(8,128)(2,1)}, bf16[3,48,8,128]{3,1,2,0:T(8,128)(2,1)S(1)}, u32[]{:S(2)}) copy-start(bf16[3,48,8,128]{3,1,2,0:T(8,128)(2,1)S(1)} %copy.179) | copy-start | bytes 884740
  76.7 19.7 %collective-permute-start.1 = (bf16[3,1,48,8,7]{4,2,3,0,1:T(8,128)(2,1)}, bf16[3,1,48,8,7]{4,2,3,0,1:T(8,128)(2,1)S(1)}, u32[]{:S(2)}, u32[]{:S(2)}) collective-permute-start(bf16[3,1,48,8,7]{4,2,3,0,1:T(8,128)(2,1)} %get-tuple-element.26), channel_id=1, source_target_pairs={{1,0},{2,1},{3,2},{4,3},{5,4},{6,5},{7,6},{9,8},{10,9},{11,10},{12... | collective-permute-start | bytes 48392 | tf_op jit(solution)/shard_map/ppermute | solution.py:17
  78.6 14.6 %collective-permute-start = (bf16[3,1,48,8,7]{4,2,3,0,1:T(8,128)(2,1)}, bf16[3,1,48,8,7]{4,2,3,0,1:T(8,128)(2,1)S(1)}, u32[]{:S(2)}, u32[]{:S(2)}) collective-permute-start(bf16[3,1,48,8,7]{4,2,3,0,1:T(8,128)(2,1)} %get-tuple-element.27), channel_id=1, source_target_pairs={{0,1},{1,2},{2,3},{3,4},{4,5},{5,6},{6,7},{8,9},{9,10},{10,11},{11... | collective-permute-start | bytes 48392 | tf_op jit(solution)/shard_map/ppermute | solution.py:15
  85.9 1.9 copy-start.1
  87.9 17.3 %collective-permute-start.4 = (bf16[2,3,1,48,7,128]{5,3,4,1,2,0:T(8,128)(2,1)S(1)}, bf16[2,3,1,48,7,128]{5,3,4,1,2,0:T(8,128)(2,1)S(1)}, u32[]{:S(2)}, u32[]{:S(2)}) collective-permute-start(bf16[2,3,1,48,7,128]{5,3,4,1,2,0:T(8,128)(2,1)S(1)} %get-tuple-element.20), channel_id=1, source_target_pairs={{0,8},{8,16},{16,24},{24,32},{32,40},{40,48},{48,56},{56,64},{64,7... | collective-permute-start | bytes 1548296 | tf_op jit(solution)/shard_map/ppermute | solution.py:15
  91.7 14.8 %collective-permute-start.5 = (bf16[2,3,1,48,7,128]{5,3,4,1,2,0:T(8,128)(2,1)S(1)}, bf16[2,3,1,48,7,128]{5,3,4,1,2,0:T(8,128)(2,1)S(1)}, u32[]{:S(2)}, u32[]{:S(2)}) collective-permute-start(bf16[2,3,1,48,7,128]{5,3,4,1,2,0:T(8,128)(2,1)S(1)} %get-tuple-element.21), channel_id=1, source_target_pairs={{8,0},{16,8},{24,16},{32,24},{40,32},{48,40},{56,48},{64,56},{72,6... | collective-permute-start | bytes 1548296 | tf_op jit(solution)/shard_map/ppermute | solution.py:17
  94.6 1.1 copy-start.7
  98.9 1.1 copy-start.4
  102.0 1.0 copy-start.3
  105.2 0.7 copy-start.13
  109.3 1.2 copy-start.11
  110.4 0.7 copy-start.14
Sparse Core Ops, SparseCore 0:
  113.7 255.4 all-reduce.3
where the time goes:
time: 379 us; the launch traced here: 378 us
  waiting for transfers between devices  267 us (70%)
  starting transfers between devices  40 us (11%)
  matrix products  33.7 us (9%)
  local copies, waits for them, and re-layouts  19.4 us (5%)
  between operations  15.2 us (4%)
    psum x1, waiting for transfers between devices, per_device(): wx_sum, wy_sum = lax.psum((wx_term, wy_term), ('gx', 'gy'))  255 us
    dot_general x60, matrix products, conv_padded(): jnp.einsum('bzcxy,co->bzoxy', piece, weight[tap], preferred_element_type=...  25.2 us
    unnamed x41, local copies, waits for them, and re-layouts  12.9 us
    all_to_all x1, starting transfers between devices, per_device(): lines = lax.all_to_all(field, 'gx', split_axis=4, concat_axis=3, tiled=True)  11.3 us
    all_to_all x1, starting transfers between devices, per_device(): lax.all_to_all(act_lines, 'gx', split_axis=3, concat_axis=4, tiled=True)  9.97 us
    ppermute x3, starting transfers between devices, with_halo(): lax.ppermute(tail, axis, [(i, (i + 1) % count) for i in range(ends)])  8.62 us
    dot_general x30, matrix products, tap_products(): jnp.einsum('bzcxy,bzoxy->co', piece, grads, preferred_element_type=jnp.fl...  8.47 us
  transfers between devices with their start and end apart: 10, of which 5 were waited for; matrix products, arithmetic and copies ran while one was open for 9% of the time, Pallas kernels for 0%

commit v1 on v0

--- a/solution.py
+++ b/solution.py
@@ -2,6 +2,12 @@
 import jax.numpy as jnp
 from jax import lax
 from jax.sharding import PartitionSpec as P
+
+
+def lead_the_routes_all(frame_in):
+    for i0 in ("gx", "gy"):
+        frame_in = jax.lax.psum(frame_in, i0)
+    return frame_in
 
 
 def with_halo(cells, sides, width):
@@ -80,7 +86,7 @@
         cotangent.astype(jnp.float32) + conv_padded(grad_xpad, flipped(weight_x), 3)
     ).astype(jnp.bfloat16)
     wx_term = tap_products(field_pad, pre_grad, taps, 3)
-    wx_sum, wy_sum = lax.psum((wx_term, wy_term), ("gx", "gy"))
+    wx_sum, wy_sum = lead_the_routes_all((wx_term, wy_term))
     count = (
         field.shape[0]
         * field.shape[1]

time: 379 us -> 339 us (0.89)
  waiting for transfers between devices: 267 us -> 225 us
    psum x1 -> x2, waiting for transfers between devices: 255 us -> 212 us  [lead_the_routes_all(): frame_in = jax.lax.psum(frame_in, i0)]
  transfers between devices with their start and end apart: 10 -> 11, of which waited for: 5 -> 6; matrix products, arithmetic and copies ran while one was open for 9% -> 10% of each run, Pallas kernels for 0% -> 0%
where the time goes in v1:
time: 339 us; the launch traced here: 336 us
  waiting for transfers between devices  225 us (66%)
  starting transfers between devices  40 us (12%)
  matrix products  33.7 us (10%)
  local copies, waits for them, and re-layouts  19.4 us (6%)
  between operations  15.2 us (4%)
    psum x2, waiting for transfers between devices, lead_the_routes_all(): frame_in = jax.lax.psum(frame_in, i0)  212 us
    dot_general x60, matrix products, conv_padded(): jnp.einsum('bzcxy,co->bzoxy', piece, weight[tap], preferred_element_type=...  25.2 us
    unnamed x41, local copies, waits for them, and re-layouts  12.9 us
    all_to_all x1, starting transfers between devices, per_device(): lines = lax.all_to_all(field, 'gx', split_axis=4, concat_axis=3, tiled=True)  11.3 us
    all_to_all x1, starting transfers between devices, per_device(): lax.all_to_all(act_lines, 'gx', split_axis=3, concat_axis=4, tiled=True)  9.96 us
    ppermute x3, starting transfers between devices, with_halo(): lax.ppermute(tail, axis, [(i, (i + 1) % count) for i in range(ends)])  8.62 us
    dot_general x30, matrix products, tap_products(): jnp.einsum('bzcxy,bzoxy->co', piece, grads, preferred_element_type=jnp.fl...  8.47 us
    all_to_all x1, waiting for transfers between devices, per_device(): lax.all_to_all(act_lines, 'gx', split_axis=3, concat_axis=4, tiled=True)  6.88 us
  transfers between devices with their start and end apart: 11, of which 6 were waited for; matrix products, arithmetic and copies ran while one was open for 10% of the time, Pallas kernels for 0%

profile of v1, /device:TPU:8, one launch (start us, length us, event | category | flops | bytes accessed | tf_op | source)
XLA Modules:
  0.0 335.9 jit_solution(2623708726200113873)
XLA Ops:
  7.2 1.6 copy.144
  8.8 1.7 reshape.644
  10.5 11.3 %all-to-all-start = ((bf16[32,2,2304]{2,1,0:T(2,128)(2,1)}), bf16[32,2,2304]{2,1,0:T(2,128)(2,1)S(1)}, u32[]{:S(2)}, u32[]{:S(2)}) async-start(bf16[32,2,2304]{2,1,0:T(2,128)(2,1)} %reshape.644), calls=%async_computation | async-start | bytes 589824 | tf_op jit(solution)/shard_map/all_to_all | solution.py:67
  22.1 1.9 collective-permute-start.3
  24.0 2.4 collective-permute-start.2
  26.7 0.7 reverse_bitcast_fusion
  27.4 0.8 copy.389
  28.2 3.9 %collective-permute-done.2 = bf16[3,1,48,8,7]{4,2,3,0,1:T(8,128)(2,1)S(1)} collective-permute-done((bf16[3,1,48,8,7]{4,2,3,0,1:T(8,128)(2,1)S(1)}, bf16[3,1,48,8,7]{4,2,3,0,1:T(8,128)(2,1)S(1)}, u32[]{:S(2)}, u32[]{:S(2)}) %collective-permute-start.2) | collective-permute-done | bytes 16160 | tf_op jit(solution)/shard_map/ppermute | solution.py:21
  35.1 1.1 fusion.6
  36.2 0.8 reshape.645
  39.8 0.4 convolution_add_fusion.39
  42.6 0.6 copy.165
  43.2 1.7 reshape.646
  44.9 10.0 %all-to-all-start.1 = ((bf16[32,2,2304]{2,1,0:T(2,128)(2,1)}), bf16[32,2,2304]{2,1,0:T(2,128)(2,1)S(1)}, u32[]{:S(2)}, u32[]{:S(2)}) async-start(bf16[32,2,2304]{2,1,0:T(2,128)(2,1)} %reshape.646), calls=%async_computation.1 | async-start | bytes 589824 | tf_op jit(solution)/shard_map/all_to_all | solution.py:72
  54.9 1.0 fusion.5
  55.9 1.0 fusion.4
  56.9 1.0 fusion.3
  57.9 0.6 copy.196
  58.5 1.7 reshape.648
  60.2 6.9 %all-to-all-done.1 = bf16[32,2,2304]{2,1,0:T(2,128)(2,1)S(1)} async-done(((bf16[32,2,2304]{2,1,0:T(2,128)(2,1)}), bf16[32,2,2304]{2,1,0:T(2,128)(2,1)S(1)}, u32[]{:S(2)}, u32[]{:S(2)}) %all-to-all-start.1) | async-done | bytes 294944 | tf_op jit(solution)/shard_map/all_to_all | solution.py:72
  67.1 4.7 %all-to-all-start.2 = ((bf16[32,2,2304]{2,1,0:T(2,128)(2,1)}), bf16[32,2,2304]{2,1,0:T(2,128)(2,1)S(1)}, u32[]{:S(2)}, u32[]{:S(2)}) async-start(bf16[32,2,2304]{2,1,0:T(2,128)(2,1)} %reshape.648), calls=%async_computation.2 | async-start | bytes 589824 | tf_op jit(solution)/shard_map/all_to_all | solution.py:73
  71.9 1.9 fusion.2
  73.7 0.8 reshape.647
  74.8 0.5 copy.168
  75.3 0.5 copy.179
  75.8 0.9 fusion.299
  76.7 1.9 collective-permute-start.1
  78.6 2.4 collective-permute-start
  81.0 1.1 fusion.178
  82.1 1.3 all-to-all-done.2
  83.4 0.8 reshape.649
  84.6 1.3 copy.202
  85.9 1.9 fusion.65
  87.9 3.8 %collective-permute-start.4 = (bf16[2,3,1,48,7,128]{5,3,4,1,2,0:T(8,128)(2,1)S(1)}, bf16[2,3,1,48,7,128]{5,3,4,1,2,0:T(8,128)(2,1)S(1)}, u32[]{:S(2)}, u32[]{:S(2)}) collective-permute-start(bf16[2,3,1,48,7,128]{5,3,4,1,2,0:T(8,128)(2,1)S(1)} %get-tuple-element.22), channel_id=1, source_target_pairs={{0,8},{8,16},{16,24},{24,32},{32,40},{40,48},{48,56},{56,64},{64,7... | collective-permute-start | bytes 1548296 | tf_op jit(solution)/shard_map/ppermute | solution.py:21
  91.7 1.5 collective-permute-start.5
  96.0 0.4 fusion.185
  100.4 0.4 convolution_add_fusion.26
  101.2 0.4 convolution_add_fusion.24
  101.6 0.4 convolution_add_fusion.23
  102.0 0.4 convolution_add_fusion.22
  102.9 0.4 fusion.23
  103.7 0.8 copy.220
  105.2 0.7 copy-done.13
  106.0 0.6 collective-permute-done.5
  113.7 149.4 %all-reduce.6.cloned.1.call-done = (f32[15,48,48]{2,1,0:T(8,128)}, f32[15,48,48]{2,1,0:T(8,128)}) async-done(((f32[15,48,48]{2,1,0:T(8,128)}, f32[15,48,48]{2,1,0:T(8,128)}), (f32[15,48,48]{2,1,0:T(8,128)}, f32[15,48,48]{2,1,0:T(8,128)})) %all-reduce.6.cloned.1.call-update) | async-done | bytes 276496 | tf_op jit(solution)/shard_map/psum | solution.py:9
  263.4 0.8 copy.221
  264.2 62.9 %all-reduce.8.cloned.1.call-done = (f32[15,48,48]{2,1,0:T(8,128)}, f32[15,48,48]{2,1,0:T(8,128)}) async-done(((f32[15,48,48]{2,1,0:T(8,128)}, f32[15,48,48]{2,1,0:T(8,128)}), (f32[15,48,48]{2,1,0:T(8,128)}, f32[15,48,48]{2,1,0:T(8,128)})) %all-reduce.8.cloned.1.call-update) | async-done | bytes 276496 | tf_op jit(solution)/shard_map/psum | solution.py:9
  327.1 2.0 broadcast_multiply_fusion
  (129 shorter events, 24.9 us)
Async XLA Ops:
  7.2 14.7 %copy-start = (bf16[3,1,48,8,128]{4,3,2,1,0:T(8,128)(2,1)S(1)}, bf16[3,1,48,8,128]{4,3,2,1,0:T(8,128)(2,1)}, u32[]{:S(2)}) copy-start(bf16[3,1,48,8,128]{4,3,2,1,0:T(8,128)(2,1)} %param.7) | copy-start | bytes 884740
  8.8 17.7 %copy-start.9 = (bf16[15,48,48]{2,1,0:T(8,128)(2,1)S(1)}, bf16[15,48,48]{2,1,0:T(8,128)(2,1)}, u32[]{:S(2)}) copy-start(bf16[15,48,48]{2,1,0:T(8,128)(2,1)} %param.6) | copy-start | bytes 207364
  10.5 25.7 %all-to-all-start = ((bf16[32,2,2304]{2,1,0:T(2,128)(2,1)}), bf16[32,2,2304]{2,1,0:T(2,128)(2,1)S(1)}, u32[]{:S(2)}, u32[]{:S(2)}) async-start(bf16[32,2,2304]{2,1,0:T(2,128)(2,1)} %reshape.644), calls=%async_computation | async-start | bytes 589824 | tf_op jit(solution)/shard_map/all_to_all | solution.py:67
  21.8 4.9 %copy-start.8 = (bf16[15,48,48]{2,1,0:T(8,128)(2,1)S(1)}, bf16[15,48,48]{2,1,0:T(8,128)(2,1)}, u32[]{:S(2)}) copy-start(bf16[15,48,48]{2,1,0:T(8,128)(2,1)} %param.5) | copy-start | bytes 207364
  21.9 5.5 %copy-start.2 = (bf16[3,1,48,8,128]{4,3,2,1,0:T(8,128)(2,1)S(1)}, bf16[3,1,48,8,128]{4,3,2,1,0:T(8,128)(2,1)}, u32[]{:S(2)}) copy-start(bf16[3,1,48,8,128]{4,3,2,1,0:T(8,128)(2,1)} %param.4) | copy-start | bytes 884740
  22.1 12.6 %collective-permute-start.3 = (bf16[3,1,48,8,7]{4,2,3,0,1:T(8,128)(2,1)S(1)}, bf16[3,1,48,8,7]{4,2,3,0,1:T(8,128)(2,1)S(1)}, u32[]{:S(2)}, u32[]{:S(2)}) collective-permute-start(bf16[3,1,48,8,7]{4,2,3,0,1:T(8,128)(2,1)S(1)} %get-tuple-element.24), channel_id=1, source_target_pairs={{1,0},{2,1},{3,2},{4,3},{5,4},{6,5},{7,6},{9,8},{10,9},{11,10},{12... | collective-permute-start | bytes 48392 | tf_op jit(solution)/shard_map/ppermute | solution.py:23
  24.0 8.0 %collective-permute-start.2 = (bf16[3,1,48,8,7]{4,2,3,0,1:T(8,128)(2,1)S(1)}, bf16[3,1,48,8,7]{4,2,3,0,1:T(8,128)(2,1)S(1)}, u32[]{:S(2)}, u32[]{:S(2)}) collective-permute-start(bf16[3,1,48,8,7]{4,2,3,0,1:T(8,128)(2,1)S(1)} %get-tuple-element.25), channel_id=1, source_target_pairs={{0,1},{1,2},{2,3},{3,4},{4,5},{5,6},{6,7},{8,9},{9,10},{10,11},{11... | collective-permute-start | bytes 48392 | tf_op jit(solution)/shard_map/ppermute | solution.py:21
  26.5 8.6 %copy-start.12 = (bf16[15,48,48]{1,2,0:T(8,128)(2,1)}, bf16[15,48,48]{1,2,0:T(8,128)(2,1)S(1)}, u32[]{:S(2)}) copy-start(bf16[15,48,48]{1,2,0:T(8,128)(2,1)S(1)} %reverse_bitcast_fusion.1) | copy-start | bytes 207364
  42.4 12.5 %copy-start.5 = (f32[48,3,8,128]{3,0,2,1:T(8,128)S(1)}, f32[48,3,8,128]{3,0,2,1:T(8,128)}, u32[]{:S(2)}) copy-start(f32[48,3,8,128]{3,0,2,1:T(8,128)} %fusion.6) | copy-start | bytes 1769476
  44.9 22.2 %all-to-all-start.1 = ((bf16[32,2,2304]{2,1,0:T(2,128)(2,1)}), bf16[32,2,2304]{2,1,0:T(2,128)(2,1)S(1)}, u32[]{:S(2)}, u32[]{:S(2)}) async-start(bf16[32,2,2304]{2,1,0:T(2,128)(2,1)} %reshape.646), calls=%async_computation.1 | async-start | bytes 589824 | tf_op jit(solution)/shard_map/all_to_all | solution.py:72
  67.1 16.3 %all-to-all-start.2 = ((bf16[32,2,2304]{2,1,0:T(2,128)(2,1)}), bf16[32,2,2304]{2,1,0:T(2,128)(2,1)S(1)}, u32[]{:S(2)}, u32[]{:S(2)}) async-start(bf16[32,2,2304]{2,1,0:T(2,128)(2,1)} %reshape.648), calls=%async_computation.2 | async-start | bytes 589824 | tf_op jit(solution)/shard_map/all_to_all | solution.py:73
  71.8 191.3 %all-reduce.6.cloned.1.call-start = ((), (), s32[]{:S(2)}) async-start(), calls=%async_computation.3 | async-start | bytes 1474560 | tf_op jit(solution)/shard_map/psum | solution.py:9
  74.8 6.2 %copy-start.10 = (bf16[15,48,48]{2,1,0:T(8,128)(2,1)S(1)}, bf16[15,48,48]{2,1,0:T(8,128)(2,1)}, u32[]{:S(2)}) copy-start(bf16[15,48,48]{2,1,0:T(8,128)(2,1)} %param.6) | copy-start | bytes 207364
  75.8 8.4 %copy-start.6 = (bf16[3,48,8,128]{3,1,2,0:T(8,128)(2,1)}, bf16[3,48,8,128]{3,1,2,0:T(8,128)(2,1)S(1)}, u32[]{:S(2)}) copy-start(bf16[3,48,8,128]{3,1,2,0:T(8,128)(2,1)S(1)} %copy.179) | copy-start | bytes 884740
  76.7 19.7 %collective-permute-start.1 = (bf16[3,1,48,8,7]{4,2,3,0,1:T(8,128)(2,1)}, bf16[3,1,48,8,7]{4,2,3,0,1:T(8,128)(2,1)S(1)}, u32[]{:S(2)}, u32[]{:S(2)}) collective-permute-start(bf16[3,1,48,8,7]{4,2,3,0,1:T(8,128)(2,1)} %get-tuple-element.28), channel_id=1, source_target_pairs={{1,0},{2,1},{3,2},{4,3},{5,4},{6,5},{7,6},{9,8},{10,9},{11,10},{12... | collective-permute-start | bytes 48392 | tf_op jit(solution)/shard_map/ppermute | solution.py:23
  78.6 14.6 %collective-permute-start = (bf16[3,1,48,8,7]{4,2,3,0,1:T(8,128)(2,1)}, bf16[3,1,48,8,7]{4,2,3,0,1:T(8,128)(2,1)S(1)}, u32[]{:S(2)}, u32[]{:S(2)}) collective-permute-start(bf16[3,1,48,8,7]{4,2,3,0,1:T(8,128)(2,1)} %get-tuple-element.29), channel_id=1, source_target_pairs={{0,1},{1,2},{2,3},{3,4},{4,5},{5,6},{6,7},{8,9},{9,10},{10,11},{11... | collective-permute-start | bytes 48392 | tf_op jit(solution)/shard_map/ppermute | solution.py:21
  85.9 1.9 copy-start.1
  87.9 17.3 %collective-permute-start.4 = (bf16[2,3,1,48,7,128]{5,3,4,1,2,0:T(8,128)(2,1)S(1)}, bf16[2,3,1,48,7,128]{5,3,4,1,2,0:T(8,128)(2,1)S(1)}, u32[]{:S(2)}, u32[]{:S(2)}) collective-permute-start(bf16[2,3,1,48,7,128]{5,3,4,1,2,0:T(8,128)(2,1)S(1)} %get-tuple-element.22), channel_id=1, source_target_pairs={{0,8},{8,16},{16,24},{24,32},{32,40},{40,48},{48,56},{56,64},{64,7... | collective-permute-start | bytes 1548296 | tf_op jit(solution)/shard_map/ppermute | solution.py:21
  91.7 14.8 %collective-permute-start.5 = (bf16[2,3,1,48,7,128]{5,3,4,1,2,0:T(8,128)(2,1)S(1)}, bf16[2,3,1,48,7,128]{5,3,4,1,2,0:T(8,128)(2,1)S(1)}, u32[]{:S(2)}, u32[]{:S(2)}) collective-permute-start(bf16[2,3,1,48,7,128]{5,3,4,1,2,0:T(8,128)(2,1)S(1)} %get-tuple-element.23), channel_id=1, source_target_pairs={{8,0},{16,8},{24,16},{32,24},{40,32},{48,40},{56,48},{64,56},{72,6... | collective-permute-start | bytes 1548296 | tf_op jit(solution)/shard_map/ppermute | solution.py:23
  94.6 1.1 copy-start.7
  98.9 1.1 copy-start.4
  102.0 1.0 copy-start.3
  105.2 0.7 copy-start.13
  109.3 1.2 copy-start.11
  110.5 0.7 copy-start.14
  113.2 213.9 %all-reduce.8.cloned.1.call-start = ((), (), s32[]{:S(2)}) async-start(), calls=%async_computation.4 | async-start | bytes 1474560 | tf_op jit(solution)/shard_map/psum | solution.py:9
Sparse Core Ops, SparseCore 0:
  113.3 149.7 all-reduce.5
  265.7 61.3 all-reduce.7
